TPU v7x, 32 devices: a whole 2x2x4 slice. The times are simulated.
32 devices in a mesh: groups: 2 (over y), seq: 4 (over x, core), fsdp: 4 (over z).
Axes of the slice: x: 2, y: 2, z: 4, core: 2. Of those that a mesh axis runs over, the one named last changes fastest.
Arguments:
- tokens: bfloat16 [16, 512, 1536], P(('groups', 'fsdp'), 'seq'), parts along dimension 0, may hold values from -6 to 6
- in_weight: bfloat16 [1536, 4608], P(None, 'fsdp'), may hold values from -0.15625 to 0.15625
- short_weight: float32 [3, 4608], replicated, may hold values from -3.5 to 3.5
- basis_in: float32 [17, 64], replicated, may hold values from -4 to 4
- basis_bias: float32 [64], replicated, may hold values from -3.140625 to 3.140625
- basis_mid: float32 [64, 64], replicated, may hold values from -1.5 to 1.5
- basis_shift: float32 [64], replicated, may hold values from -3.140625 to 3.140625
- response_out: float32 [2, 64, 1536], P(None, None, 'fsdp'), may hold values from -0.0234375 to 0.0234375
- skip_gain: float32 [1536], P('fsdp'), may hold values from -4 to 4
- block_counts: int32 [16, 4], P(('groups', 'fsdp'), 'seq'), parts along dimension 0, may hold values from 1 to 128, as said below
Outputs:
- mixed: bfloat16 [16, 512, 1536], P(('groups', 'fsdp'), 'seq'), parts along dimension 0
There are 2 independent parts, one for each index of `groups`. A program takes and returns all parts, laid end to end along the dimension named above; an argument that names none is the same for every part. Nothing has to cross between parts.
Inputs may be any that keep to these rules, and one draw needn't show every extreme that they name: `block_counts`: in every table one block holds all 128 tokens and another holds a single token.
All inputs are finite; a program needn't handle non-finite values.
Results may differ from a plain program's by a relative error of at most 0.007.
Values may be sent and summed in bfloat16 or wider, within the bound.
No kernel may reach another device: no remote copies, remote signals or barrier semaphores. Data moves between devices by JAX's collectives and lax.ppermute only.
A program may use at most 128 MiB of HBM per device.

v0:
```python
import jax
import jax.numpy as jnp
from jax import lax
from jax.sharding import PartitionSpec as P


def padded_2(cells, sides, width):
    for axis, dim in sides:
        count = lax.axis_size(axis)
        ends = count - 1
        head = lax.slice_in_dim(cells, 0, width, axis=dim)
        tail = lax.slice_in_dim(cells, cells.shape[dim] - width, cells.shape[dim], axis=dim)
        cells = jnp.concatenate(
            [
                lax.ppermute(tail, axis, [(i, (i + 1) % count) for i in range(ends)]),
                cells,
                lax.ppermute(head, axis, [((i + 1) % count, i) for i in range(ends)]),
            ],
            axis=dim,
        )
    return cells


def filter_basis(lag_values, total_len, basis_in, basis_bias, basis_mid, basis_shift):
    band_count = (basis_in.shape[0] - 1) // 2
    distance = jnp.abs(lag_values)
    periods = (2 ** (jnp.arange(band_count, dtype=jnp.int32) + 2) + 1).astype(jnp.int32)
    angles = (
        2.0
        * jnp.pi
        * (distance[:, None] % periods[None, :]).astype(jnp.float32)
        / periods[None, :].astype(jnp.float32)
    )
    linear = distance.astype(jnp.float32)[:, None] / total_len
    encoded = jnp.concatenate([linear, jnp.cos(angles), jnp.sin(angles)], axis=1)
    hidden = jnp.sin(jnp.dot(encoded, basis_in, precision=lax.Precision.HIGHEST) + basis_bias)
    return jnp.sin(jnp.dot(hidden, basis_mid, precision=lax.Precision.HIGHEST) + basis_shift)


def forward_table(block_len):
    period = 2 * block_len
    frequency = jnp.arange(block_len, dtype=jnp.int32)[:, None]
    samples = jnp.arange(period, dtype=jnp.int32)[None, :]
    phases = 2.0 * jnp.pi / period * (frequency * samples % period).astype(jnp.float32)
    alternate = (1 - 2 * (samples % 2)).astype(jnp.float32)
    real_rows = jnp.cos(phases)
    imag_rows = jnp.where(frequency == 0, alternate, -jnp.sin(phases))
    return jnp.concatenate([real_rows, imag_rows], axis=0)


def inverse_table(block_len):
    period = 2 * block_len
    places = jnp.arange(block_len, dtype=jnp.int32)[:, None]
    frequency = jnp.arange(block_len, dtype=jnp.int32)[None, :]
    phases = 2.0 * jnp.pi / period * (places * frequency % period).astype(jnp.float32)
    alternate = (1 - 2 * (places % 2)).astype(jnp.float32)
    real_cols = jnp.where(frequency == 0, 1.0, 2.0 * jnp.cos(phases)) / period
    imag_cols = jnp.where(frequency == 0, alternate, -2.0 * jnp.sin(phases)) / period
    return jnp.concatenate([real_cols, imag_cols], axis=1)


def packed_product(response, signal, block_len):
    first_slot = (jnp.arange(block_len) == 0)[:, None]
    resp_real = response[..., :block_len, :]
    resp_imag = response[..., block_len:, :]
    sig_real = signal[..., :block_len, :]
    sig_imag = signal[..., block_len:, :]
    cross_term = resp_imag * sig_imag
    prod_real = resp_real * sig_real - jnp.where(first_slot, 0.0, cross_term)
    prod_imag = jnp.where(first_slot, cross_term, resp_real * sig_imag + resp_imag * sig_real)
    return jnp.concatenate([prod_real, prod_imag], axis=-2)


def shards(
    tokens,
    in_weight,
    short_weight,
    basis_in,
    basis_bias,
    basis_mid,
    basis_shift,
    response_out,
    skip_gain,
    block_counts,
):
    seq_dev, block_len, width = tokens.shape
    group_tokens = lax.all_gather(tokens, "fsdp", axis=0, tiled=True)
    group_rows = group_tokens.shape[0]
    local_cols = in_weight.shape[1]
    partial = jnp.dot(
        group_tokens.reshape(group_rows * block_len, width),
        in_weight,
        preferred_element_type=jnp.float32,
    ).astype(jnp.bfloat16)
    partial = partial.reshape(group_rows, block_len, local_cols)
    projected = lax.all_to_all(partial, "fsdp", 0, 2, tiled=True)
    padded = padded_2(projected, (("seq", 1),), 1)
    shorted = (
        short_weight[0] * padded[:, :-2]
        + short_weight[1] * padded[:, 1:-1]
        + short_weight[2] * padded[:, 2:]
    )
    query_gate = shorted[:, :, :width]
    key_part = shorted[:, :, width : 2 * width]
    value_part = shorted[:, :, 2 * width :]
    valid_mask = (jnp.arange(block_len, dtype=jnp.int32)[None, :] < block_counts).astype(
        jnp.float32
    )
    carried = (key_part * value_part * valid_mask[:, :, None]).astype(jnp.bfloat16)
    full_out, full_skip = (
        lax.all_gather(response_out, "fsdp", axis=2, tiled=True),
        lax.all_gather(skip_gain, "fsdp", axis=0, tiled=True),
    )
    stacked_out = full_out.reshape(2 * full_out.shape[1], width)
    seq_count = lax.axis_size("seq")
    position = lax.axis_index("seq")
    total_len = float(seq_count * block_len)
    forward = forward_table(block_len)
    forward_half = forward[:, :block_len]
    inverse = inverse_table(block_len)
    circular = jnp.arange(2 * block_len, dtype=jnp.int32)
    wrapped = jnp.where(circular < block_len, circular, circular - 2 * block_len)

    def kernel_response(offset, out_cols):
        lag_values = offset + wrapped
        basis_rows = filter_basis(
            lag_values, total_len, basis_in, basis_bias, basis_mid, basis_shift
        )
        ahead_mask = (lag_values >= 0).astype(jnp.float32)[:, None]
        paired = jnp.concatenate([basis_rows * ahead_mask, basis_rows * (1.0 - ahead_mask)], axis=1)
        return jnp.dot(
            jnp.dot(forward, paired, precision=lax.Precision.HIGHEST),
            out_cols,
            precision=lax.Precision.HIGHEST,
        )

    def add_block(spectrum, block_rows, start):
        offset = position * block_len - start
        response = kernel_response(offset, stacked_out)
        signal = jnp.einsum(
            "fc,scd->sfd",
            forward_half,
            block_rows.astype(jnp.float32),
            precision=lax.Precision.HIGHEST,
        )
        return spectrum + packed_product(response[None], signal, block_len)

    initial = jnp.zeros((seq_dev, 2 * block_len, width), jnp.float32)
    piece = lax.all_gather(carried, "seq", axis=1, tiled=True)
    piece_rows = piece.shape[1]
    block_total = piece_rows // block_len

    def one_block(block_index, carry):
        block_rows = lax.dynamic_slice_in_dim(piece, block_index * block_len, block_len, 1)
        return add_block(carry, block_rows, block_index * block_len)

    spectrum = lax.fori_loop(0, block_total, one_block, initial)
    conv = jnp.einsum("if,sfd->sid", inverse, spectrum, precision=lax.Precision.HIGHEST)
    return (query_gate * (conv + full_skip * carried.astype(jnp.float32))).astype(jnp.bfloat16)


def solution(mesh):
    placed = (
        P(("groups", "fsdp"), "seq", None),
        P(None, "fsdp"),
        P(),
        P(),
        P(),
        P(),
        P(),
        P(None, None, "fsdp"),
        P("fsdp"),
        P(("groups", "fsdp"), "seq"),
    )
    return jax.shard_map(
        shards,
        mesh=mesh,
        in_specs=placed,
        out_specs=P(("groups", "fsdp"), "seq", None),
        check_vma=False,
    )
```

profile of v0, /device:TPU:2, one launch (start us, length us, event | category | flops | bytes accessed | tf_op | source)
XLA Modules:
  0.0 302.2 jit_solution(2501134679842409714)
XLA Ops:
  7.3 66.4 %all-gather.4.cloned.1.call-done = bf16[8,128,1536]{2,1,0:T(8,128)(2,1)} async-done(((bf16[2,128,1536]{2,1,0:T(8,128)(2,1)}), bf16[8,128,1536]{2,1,0:T(8,128)(2,1)}) %all-gather.4.cloned.1.call-update) | async-done | bytes 3145744 | tf_op jit(solution)/shard_map/all_gather | solution.py:87
  73.7 7.6 %convolution_convert_fusion = bf16[1024,1152]{1,0:T(8,128)(2,1)} fusion(bf16[1024,1536]{1,0:T(8,128)(2,1)} %bitcast.65, bf16[1536,1152]{1,0:T(8,128)(2,1)S(1)} %copy-done), kind=kOutput, calls=%fused_computation.58 | convolution fusion | flops 3625058304 | bytes 9043968 | tf_op jit(solution)/shard_map/dot_general | solution.py:90
  81.3 4.6 %all-to-all-start = ((bf16[8,128,1152]{2,1,0:T(8,128)(2,1)}), bf16[8,128,1152]{2,1,0:T(8,128)(2,1)}, u32[]{:S(2)}, u32[]{:S(2)}) async-start(bf16[8,128,1152]{2,1,0:T(8,128)(2,1)} %bitcast.63), calls=%async_computation | async-start | bytes 4718592 | tf_op jit(solution)/shard_map/all_to_all | solution.py:96
  86.0 54.0 %all-to-all-done = bf16[8,128,1152]{2,1,0:T(8,128)(2,1)} async-done(((bf16[8,128,1152]{2,1,0:T(8,128)(2,1)}), bf16[8,128,1152]{2,1,0:T(8,128)(2,1)}, u32[]{:S(2)}, u32[]{:S(2)}) %all-to-all-start) | async-done | bytes 2359328 | tf_op jit(solution)/shard_map/all_to_all | solution.py:96
  140.0 4.3 %copy.20 = bf16[4,2,128,1152]{2,3,0,1:T(8,128)(2,1)} copy(bf16[4,2,128,1152]{3,2,1,0:T(8,128)(2,1)} %bitcast.2) | data formatting | bytes 4718592 | tf_op jit(solution)/shard_map/all_to_all | solution.py:96
  144.3 5.3 %fusion.56 = (bf16[2,1,4608]{1,2,0:T(8,128)(2,1)}, bf16[2,1,4608]{1,2,0:T(8,128)(2,1)}) fusion(bf16[2,128,4608]{1,2,0:T(8,128)(2,1)} %bitcast.60), kind=kLoop, calls=%fused_computation.111 | loop fusion | bytes 73728 | tf_op jit(solution)/shard_map/slice | solution.py:12
  149.6 2.7 copy.21
  154.2 2.7 copy.23
  156.9 3.6 %collective-permute-start.1 = (bf16[2,1,4608]{2,0,1:T(2,128)(2,1)}, bf16[2,1,4608]{2,0,1:T(2,128)(2,1)}, u32[]{:S(2)}, u32[]{:S(2)}) collective-permute-start(bf16[2,1,4608]{2,0,1:T(2,128)(2,1)} %copy.23), channel_id=1, source_target_pairs={{4,0},{8,4},{12,8},{5,1},{9,5},{13,9},{6,2},{10,6},{14,10},{7,3},{... | collective-permute-start | bytes 55304 | tf_op jit(solution)/shard_map/ppermute | solution.py:17
  162.3 2.6 copy.22
  164.9 2.6 copy.24
  167.6 7.7 %multiply_add_fusion = f32[2,128,4608]{1,2,0:T(8,128)S(1)} fusion(bf16[2,128,4608]{1,2,0:T(8,128)(2,1)} %bitcast.61, bf16[2,1,4608]{1,2,0:T(8,128)(2,1)} %copy.24, bf16[2,1,4608]{1,2,0:T(8,128)(2,1)} %copy.22, f32[4608]{0:T(1024)} %get-tuple-element.353, f32[4608]{0:T(1024)} %get-tuple-element.354, f32[4608]{0:T(1024)} %get-tuple-element.352), kind=kLoop, calls=%fused_computation.57 | loop fusion | flops 16515072 | bytes 7170048 | tf_op jit(solution)/shard_map/add | solution.py:99
  178.5 11.9 %all-gather = f32[4,1,384]{2,1,0:T(1,128)S(1)} all-gather(f32[1,1,384]{2,1,0:T(1,128)S(1)} %reshape.183), channel_id=1, replica_groups=mesh['groups'=2,'seq'=4,'fsdp'=4] {'fsdp'}, dimensions={0}, use_global_device_ids=true | all-gather | bytes 7680 | tf_op jit(solution)/shard_map/all_gather | solution.py:112
  193.3 18.5 %all_gather.13 = f32[2,64,1536]{2,1,0:T(8,128)} all-gather(f32[2,64,384]{2,1,0:T(8,128)} %param.19), channel_id=1, replica_groups=mesh['groups'=2,'seq'=4,'fsdp'=4] {'fsdp'}, dimensions={2}, use_global_device_ids=true | all-gather | bytes 983040 | tf_op jit(solution)/shard_map/all_gather | solution.py:111
  211.8 72.5 %while.16 = (s32[]{:T(128)}, f32[2,256,1536]{2,1,0:T(8,128)}, s32[]{:T(128)}, f32[17,64]{1,0:T(8,128)}, f32[64]{0:T(128)}, /*index=5*/f32[64,64]{1,0:T(8,128)}, ...) while((s32[]{:T(128)}, f32[2,256,1536]{2,1,0:T(8,128)}, ...), condition=%wide.region_1.2_spmd.clone, body=%wide.region_0.1_spmd.clone.sunk | while | flops 1934166400 | bytes 34141608 | solution.py:157
  219.8 2.7 convolution_bitcast_fusion.5
  225.0 4.3 %maximum_add_fusion.2 = f32[2,256,1536]{2,1,0:T(8,128)} fusion(f32[2,128,1536]{2,1,0:T(8,128)} %get-tuple-element.484, f32[2,128,1536]{2,1,0:T(8,128)} %get-tuple-element.485, f32[2,256,1536]{2,1,0:T(8,128)} %get-tuple-element.502, pred[]{:T(512)S(6)} %compare.7), kind=kLoop, calls=%fused_computation.2.clone.1 | loop fusion | flops 2359296 | bytes 9437185 | tf_op jit(solution)/shard_map/while/body/eval_jaxpr/add | solution.py:146
  237.2 2.7 convolution_bitcast_fusion.5
  242.4 5.2 %maximum_add_fusion.2 = f32[2,256,1536]{2,1,0:T(8,128)} fusion(f32[2,128,1536]{2,1,0:T(8,128)} %get-tuple-element.484, f32[2,128,1536]{2,1,0:T(8,128)} %get-tuple-element.485, f32[2,256,1536]{2,1,0:T(8,128)} %get-tuple-element.502, pred[]{:T(512)S(6)} %compare.7), kind=kLoop, calls=%fused_computation.2.clone.1 | loop fusion | flops 2359296 | bytes 9437185 | tf_op jit(solution)/shard_map/while/body/eval_jaxpr/add | solution.py:146
  255.6 2.7 convolution_bitcast_fusion.5
  260.7 5.2 %maximum_add_fusion.2 = f32[2,256,1536]{2,1,0:T(8,128)} fusion(f32[2,128,1536]{2,1,0:T(8,128)} %get-tuple-element.484, f32[2,128,1536]{2,1,0:T(8,128)} %get-tuple-element.485, f32[2,256,1536]{2,1,0:T(8,128)} %get-tuple-element.502, pred[]{:T(512)S(6)} %compare.7), kind=kLoop, calls=%fused_computation.2.clone.1 | loop fusion | flops 2359296 | bytes 9437185 | tf_op jit(solution)/shard_map/while/body/eval_jaxpr/add | solution.py:146
  273.9 2.7 convolution_bitcast_fusion.5
  279.1 5.2 %maximum_add_fusion.2 = f32[2,256,1536]{2,1,0:T(8,128)} fusion(f32[2,128,1536]{2,1,0:T(8,128)} %get-tuple-element.484, f32[2,128,1536]{2,1,0:T(8,128)} %get-tuple-element.485, f32[2,256,1536]{2,1,0:T(8,128)} %get-tuple-element.502, pred[]{:T(512)S(6)} %compare.7), kind=kLoop, calls=%fused_computation.2.clone.1 | loop fusion | flops 2359296 | bytes 9437185 | tf_op jit(solution)/shard_map/while/body/eval_jaxpr/add | solution.py:146
  284.3 8.8 %fusion.32 = bf16[2,128,1536]{1,2,0:T(8,128)(2,1)} fusion(f32[2,128,4608]{1,2,0:T(8,128)} %copy-done.3, f32[2,256,1536]{2,1,0:T(8,128)} %get-tuple-element.280, bf16[2,128,1536]{1,2,0:T(8,128)(2,1)} %fusion.31, f32[1536]{0:T(1024)S(1)} %reshape.184, f32[128,128]{1,0:T(8,128)} %get-tuple-element.392, f32[128,128]{1,0:T(8,128)} %get-tuple-element.391), kind=kOutput, calls=%fused_computation.67 | convolution fusion | flops 1209958400 | bytes 6428672 | tf_op jit(solution)/shard_map/if,sfd->sid/dot_general | solution.py:158
  (99 shorter events, 54.5 us)
Async XLA Ops:
  6.5 67.2 %copy-start = (bf16[1536,1152]{1,0:T(8,128)(2,1)S(1)}, bf16[1536,1152]{1,0:T(8,128)(2,1)}, u32[]{:S(2)}) copy-start(bf16[1536,1152]{1,0:T(8,128)(2,1)} %param.13) | copy-start | bytes 10616836
  6.5 67.2 %all-gather.4.cloned.1.call-start = ((), (), s32[]{:S(2)}) async-start(), calls=%async_computation.1 | async-start | bytes 3932160 | tf_op jit(solution)/shard_map/all_gather | solution.py:87
  81.3 4.7 %copy-start.5 = (s32[2,1]{0,1:T(1,128)S(1)}, s32[2,1]{0,1:T(1,128)}, u32[]{:S(2)}) copy-start(s32[2,1]{0,1:T(1,128)} %param.21) | copy-start | bytes 28
  81.3 58.8 %all-to-all-start = ((bf16[8,128,1152]{2,1,0:T(8,128)(2,1)}), bf16[8,128,1152]{2,1,0:T(8,128)(2,1)}, u32[]{:S(2)}, u32[]{:S(2)}) async-start(bf16[8,128,1152]{2,1,0:T(8,128)(2,1)} %bitcast.63), calls=%async_computation | async-start | bytes 4718592 | tf_op jit(solution)/shard_map/all_to_all | solution.py:96
  85.9 125.9 %all-gather.6.cloned.1.call-start = ((), (), s32[]{:S(2)}) async-start(), calls=%async_computation.2 | async-start | bytes 3932160 | tf_op jit(solution)/shard_map/all_gather | solution.py:149
  152.3 10.0 %collective-permute-start = (bf16[2,1,4608]{2,0,1:T(2,128)(2,1)}, bf16[2,1,4608]{2,0,1:T(2,128)(2,1)}, u32[]{:S(2)}, u32[]{:S(2)}) collective-permute-start(bf16[2,1,4608]{2,0,1:T(2,128)(2,1)} %copy.21), channel_id=1, source_target_pairs={{0,4},{4,8},{8,12},{1,5},{5,9},{9,13},{2,6},{6,10},{10,14},{3,7},{... | collective-permute-start | bytes 55304 | tf_op jit(solution)/shard_map/ppermute | solution.py:15
  156.9 8.0 %collective-permute-start.1 = (bf16[2,1,4608]{2,0,1:T(2,128)(2,1)}, bf16[2,1,4608]{2,0,1:T(2,128)(2,1)}, u32[]{:S(2)}, u32[]{:S(2)}) collective-permute-start(bf16[2,1,4608]{2,0,1:T(2,128)(2,1)} %copy.23), channel_id=1, source_target_pairs={{4,0},{8,4},{12,8},{5,1},{9,5},{13,9},{6,2},{10,6},{14,10},{7,3},{... | collective-permute-start | bytes 55304 | tf_op jit(solution)/shard_map/ppermute | solution.py:17
  175.2 2.1 copy-start.3
  177.4 1.1 copy-start.4
  219.8 2.7 copy-start.1
  219.8 2.7 copy-start.2
  237.2 2.7 copy-start.1
  237.2 2.7 copy-start.2
  255.6 2.7 copy-start.1
  255.6 2.7 copy-start.2
  273.9 2.7 copy-start.1
  273.9 2.7 copy-start.2
Sparse Core Ops, SparseCore 0:
  8.9 64.7 all-gather.3
  178.6 26.8 all-gather.5
where the time goes:
time: 304 us; the launch traced here: 302 us
  waiting for transfers between devices  121 us (40%)
  matrix products  52.3 us (17%)
  other arithmetic  42.7 us (14%)
  local copies, waits for them, and re-layouts  31.5 us (10%)
  blocking collectives  30.4 us (10%)
  between operations  13.5 us (4%)
  starting transfers between devices  10.2 us (3%)
    all_gather x1, waiting for transfers between devices, shards(): group_tokens = lax.all_gather(tokens, 'fsdp', axis=0, tiled=True)  66.4 us
    all_to_all x1, waiting for transfers between devices, shards(): projected = lax.all_to_all(partial, 'fsdp', 0, 2, tiled=True)  54 us
    add x4, other arithmetic, add_block(): return spectrum + packed_product(response[None], signal, block_len)  19.9 us
    all_gather x1, blocking collectives, shards(): lax.all_gather(response_out, 'fsdp', axis=2, tiled=True)  18.5 us
    all_gather x1, blocking collectives, shards(): lax.all_gather(skip_gain, 'fsdp', axis=0, tiled=True)  11.9 us
    dot_general x4, matrix products, add_block(): jnp.einsum('fc,scd->sfd', forward_half, block_rows.astype(jnp.float32), p...  10.7 us
    dot_general x4, matrix products, kernel_response(): jnp.dot(jnp.dot(forward, paired, precision=lax.Precision.HIGHEST), out_co...  10.3 us
    sub x4, other arithmetic, packed_product(): prod_real = resp_real * sig_real - jnp.where(first_slot, 0.0, cross_term)  9.89 us
  transfers between devices with their start and end apart: 5, of which 2 were waited for; matrix products, arithmetic and copies ran while one was open for 3% of the time, Pallas kernels for 0%

commit v1 on v0

--- a/solution.py
+++ b/solution.py
@@ -2,6 +2,28 @@
 import jax.numpy as jnp
 from jax import lax
 from jax.sharding import PartitionSpec as P
+
+
+def joined_along(blocks, dim):
+    shape = list(blocks.shape[1:])
+    shape[dim] *= blocks.shape[0]
+    return jnp.moveaxis(blocks, 0, dim).reshape(shape)
+
+
+def gather_around(array, axis, dim):
+    size = lax.axis_size(axis)
+    pairs = [(i, (i + 1) % size) for i in range(size)]
+    back = [(b, a) for a, b in pairs]
+    lower, upper = ([], [])
+    for step in range(size - 1):
+        if step % 2 == 0:
+            lower.append(lax.ppermute(lower[-1] if lower else array, axis, pairs))
+        else:
+            upper.append(lax.ppermute(upper[-1] if upper else array, axis, back))
+    parts = jnp.stack([*lower[::-1], array, *upper])
+    shift = lax.axis_index(axis) - len(lower)
+    parts = parts[(jnp.arange(size) - shift) % size]
+    return joined_along(parts, dim)
 
 
 def padded_2(cells, sides, width):
@@ -84,7 +106,7 @@
     block_counts,
 ):
     seq_dev, block_len, width = tokens.shape
-    group_tokens = lax.all_gather(tokens, "fsdp", axis=0, tiled=True)
+    group_tokens = gather_around(tokens, "fsdp", 0)
     group_rows = group_tokens.shape[0]
     local_cols = in_weight.shape[1]
     partial = jnp.dot(

time: 304 us -> 297 us (0.977)
  waiting for transfers between devices: 121 us -> 103 us
  local copies, waits for them, and re-layouts: 31.5 us -> 35.9 us
  starting transfers between devices: 10.2 us -> 14 us
  other arithmetic: 42.7 us -> 46 us
    all_gather x1 -> x0, waiting for transfers between devices: 66.4 us -> none  [shards(): group_tokens = lax.all_gather(tokens, 'fsdp', axis=0, tiled=True)]
    ppermute x0 -> x3, waiting for transfers between devices: none -> 51.3 us  [the longest x2 35.7 us: gather_around(): lower.append(lax.ppermute(lower[-1] if lower else array, axis, pairs))]
    gather x0 -> x1, local copies, waits for them, and re-layouts: none -> 4.31 us  [gather_around(): parts = parts[(jnp.arange(size) - shift) % size]]
    ppermute x0 -> x3, starting transfers between devices: none -> 3.83 us  [the longest x1 2.25 us: gather_around(): upper.append(lax.ppermute(upper[-1] if upper else array, axis, back))]
    another operation x0 -> x1, other arithmetic: none -> 3.22 us  [gather_around(): parts = jnp.stack([*lower[::-1], array, *upper])]
  transfers between devices with their start and end apart: 5 -> 7, of which waited for: 2 -> 4; matrix products, arithmetic and copies ran while one was open for 3% -> 3% of each run, Pallas kernels for 0% -> 0%
where the time goes in v1:
time: 297 us; the launch traced here: 295 us
  waiting for transfers between devices  103 us (35%)
  matrix products  52.3 us (18%)
  other arithmetic  46 us (15%)
  local copies, waits for them, and re-layouts  35.9 us (12%)
  blocking collectives  30.4 us (10%)
  starting transfers between devices  14 us (5%)
  between operations  13.5 us (5%)
    all_to_all x1, waiting for transfers between devices, shards(): projected = lax.all_to_all(partial, 'fsdp', 0, 2, tiled=True)  51.6 us
    ppermute x2, waiting for transfers between devices, gather_around(): lower.append(lax.ppermute(lower[-1] if lower else array, axis, pairs))  35.7 us
    add x4, other arithmetic, add_block(): return spectrum + packed_product(response[None], signal, block_len)  19.9 us
    all_gather x1, blocking collectives, shards(): lax.all_gather(response_out, 'fsdp', axis=2, tiled=True)  18.5 us
    ppermute x1, waiting for transfers between devices, gather_around(): upper.append(lax.ppermute(upper[-1] if upper else array, axis, back))  15.6 us
    all_gather x1, blocking collectives, shards(): lax.all_gather(skip_gain, 'fsdp', axis=0, tiled=True)  11.9 us
    dot_general x4, matrix products, add_block(): jnp.einsum('fc,scd->sfd', forward_half, block_rows.astype(jnp.float32), p...  10.7 us
    dot_general x4, matrix products, kernel_response(): jnp.dot(jnp.dot(forward, paired, precision=lax.Precision.HIGHEST), out_co...  10.3 us
  transfers between devices with their start and end apart: 7, of which 4 were waited for; matrix products, arithmetic and copies ran while one was open for 3% of the time, Pallas kernels for 0%

profile of v1, /device:TPU:2, one launch (start us, length us, event | category | flops | bytes accessed | tf_op | source)
XLA Modules:
  0.0 295.4 jit_solution(6264649592665230180)
XLA Ops:
  10.4 18.8 %collective-permute-done = bf16[2,128,1536]{2,1,0:T(8,128)(2,1)} collective-permute-done((bf16[2,128,1536]{2,1,0:T(8,128)(2,1)}, bf16[2,128,1536]{2,1,0:T(8,128)(2,1)}, u32[]{:S(2)}, u32[]{:S(2)}) %collective-permute-start) | collective-permute-done | bytes 786464 | tf_op jit(solution)/shard_map/ppermute | solution.py:20
  29.1 15.6 %collective-permute-done.2 = bf16[2,128,1536]{2,1,0:T(8,128)(2,1)} collective-permute-done((bf16[2,128,1536]{2,1,0:T(8,128)(2,1)}, bf16[2,128,1536]{2,1,0:T(8,128)(2,1)}, u32[]{:S(2)}, u32[]{:S(2)}) %collective-permute-start.2) | collective-permute-done | bytes 786464 | tf_op jit(solution)/shard_map/ppermute | solution.py:22
  44.8 17.0 %collective-permute-done.1 = bf16[2,128,1536]{2,1,0:T(8,128)(2,1)} collective-permute-done((bf16[2,128,1536]{2,1,0:T(8,128)(2,1)}, bf16[2,128,1536]{2,1,0:T(8,128)(2,1)}, u32[]{:S(2)}, u32[]{:S(2)}) %collective-permute-start.1) | collective-permute-done | bytes 786464 | tf_op jit(solution)/shard_map/ppermute | solution.py:20
  61.7 3.2 %pad_maximum_fusion = bf16[4,2,128,1536]{3,2,1,0:T(8,128)(2,1)} fusion(bf16[1,2,128,1536]{3,2,1,0:T(8,128)(2,1)} %bitcast.3, bf16[1,2,128,1536]{3,2,1,0:T(8,128)(2,1)} %bitcast.71, bf16[1,2,128,1536]{3,2,1,0:T(8,128)(2,1)} %bitcast.1, bf16[1,2,128,1536]{3,2,1,0:T(8,128)(2,1)} %bitcast), kind=kLoop, calls=%fused_computation.60 | loop fusion | flops 4718592 | bytes 6291456 | tf_op jit(solution)/shard_map/stack | solution.py:23
  65.0 4.3 %gather_fusion = bf16[4,2,128,1536]{3,2,1,0:T(8,128)(2,1)} fusion(bf16[4,2,128,1536]{3,2,1,0:T(8,128)(2,1)} %pad_maximum_fusion, s32[1024]{0:T(1024)S(1)} %pad_clamp_fusion), kind=kCustom, calls=%fused_computation | custom fusion | bytes 6291472 | tf_op jit(solution)/shard_map/gather | solution.py:25
  69.3 7.5 %convolution_convert_fusion = bf16[1024,1152]{1,0:T(8,128)(2,1)} fusion(bf16[1024,1536]{1,0:T(8,128)(2,1)} %bitcast.69, bf16[1536,1152]{1,0:T(8,128)(2,1)S(1)} %copy-done), kind=kOutput, calls=%fused_computation.59 | convolution fusion | flops 3625058304 | bytes 9043968 | tf_op jit(solution)/shard_map/dot_general | solution.py:112
  76.8 4.6 %all-to-all-start = ((bf16[8,128,1152]{2,1,0:T(8,128)(2,1)}), bf16[8,128,1152]{2,1,0:T(8,128)(2,1)}, u32[]{:S(2)}, u32[]{:S(2)}) async-start(bf16[8,128,1152]{2,1,0:T(8,128)(2,1)} %bitcast.70), calls=%async_computation | async-start | bytes 4718592 | tf_op jit(solution)/shard_map/all_to_all | solution.py:118
  81.6 51.6 %all-to-all-done = bf16[8,128,1152]{2,1,0:T(8,128)(2,1)} async-done(((bf16[8,128,1152]{2,1,0:T(8,128)(2,1)}), bf16[8,128,1152]{2,1,0:T(8,128)(2,1)}, u32[]{:S(2)}, u32[]{:S(2)}) %all-to-all-start) | async-done | bytes 2359328 | tf_op jit(solution)/shard_map/all_to_all | solution.py:118
  133.2 4.3 %copy.20 = bf16[4,2,128,1152]{2,3,0,1:T(8,128)(2,1)} copy(bf16[4,2,128,1152]{3,2,1,0:T(8,128)(2,1)} %bitcast.7) | data formatting | bytes 4718592 | tf_op jit(solution)/shard_map/all_to_all | solution.py:118
  137.6 5.3 %fusion.58 = (bf16[2,1,4608]{1,2,0:T(8,128)(2,1)}, bf16[2,1,4608]{1,2,0:T(8,128)(2,1)}) fusion(bf16[2,128,4608]{1,2,0:T(8,128)(2,1)} %bitcast.66), kind=kLoop, calls=%fused_computation.120 | loop fusion | bytes 73728 | tf_op jit(solution)/shard_map/slice | solution.py:34
  142.8 2.7 copy.21
  147.4 2.7 copy.23
  150.1 3.6 %collective-permute-start.4 = (bf16[2,1,4608]{2,0,1:T(2,128)(2,1)}, bf16[2,1,4608]{2,0,1:T(2,128)(2,1)}, u32[]{:S(2)}, u32[]{:S(2)}) collective-permute-start(bf16[2,1,4608]{2,0,1:T(2,128)(2,1)} %copy.23), channel_id=1, source_target_pairs={{4,0},{8,4},{12,8},{5,1},{9,5},{13,9},{6,2},{10,6},{14,10},{7,3},{... | collective-permute-start | bytes 55304 | tf_op jit(solution)/shard_map/ppermute | solution.py:39
  160.8 7.7 %multiply_add_fusion = f32[2,128,4608]{1,2,0:T(8,128)S(1)} fusion(bf16[2,128,4608]{1,2,0:T(8,128)(2,1)} %bitcast.67, bf16[2,1,4608]{1,2,0:T(8,128)(2,1)} %copy.24, bf16[2,1,4608]{1,2,0:T(8,128)(2,1)} %copy.22, f32[4608]{0:T(1024)} %get-tuple-element.353, f32[4608]{0:T(1024)} %get-tuple-element.354, f32[4608]{0:T(1024)} %get-tuple-element.352), kind=kLoop, calls=%fused_computation.58 | loop fusion | flops 16515072 | bytes 7170048 | tf_op jit(solution)/shard_map/add | solution.py:121
  171.7 11.9 %all-gather = f32[4,1,384]{2,1,0:T(1,128)S(1)} all-gather(f32[1,1,384]{2,1,0:T(1,128)S(1)} %reshape.236), channel_id=1, replica_groups=mesh['groups'=2,'seq'=4,'fsdp'=4] {'fsdp'}, dimensions={0}, use_global_device_ids=true | all-gather | bytes 7680 | tf_op jit(solution)/shard_map/all_gather | solution.py:134
  186.5 18.5 %all_gather.9 = f32[2,64,1536]{2,1,0:T(8,128)} all-gather(f32[2,64,384]{2,1,0:T(8,128)} %param.19), channel_id=1, replica_groups=mesh['groups'=2,'seq'=4,'fsdp'=4] {'fsdp'}, dimensions={2}, use_global_device_ids=true | all-gather | bytes 983040 | tf_op jit(solution)/shard_map/all_gather | solution.py:133
  205.1 72.5 %while.16 = (s32[]{:T(128)}, f32[2,256,1536]{2,1,0:T(8,128)}, s32[]{:T(128)}, f32[17,64]{1,0:T(8,128)}, f32[64]{0:T(128)}, /*index=5*/f32[64,64]{1,0:T(8,128)}, ...) while((s32[]{:T(128)}, f32[2,256,1536]{2,1,0:T(8,128)}, ...), condition=%wide.region_1.2_spmd.clone, body=%wide.region_0.1_spmd.clone.sunk | while | flops 1934166400 | bytes 34141608 | solution.py:179
  218.2 4.3 %maximum_add_fusion.2 = f32[2,256,1536]{2,1,0:T(8,128)} fusion(f32[2,128,1536]{2,1,0:T(8,128)} %get-tuple-element.484, f32[2,128,1536]{2,1,0:T(8,128)} %get-tuple-element.485, f32[2,256,1536]{2,1,0:T(8,128)} %get-tuple-element.502, pred[]{:T(512)S(6)} %compare.14), kind=kLoop, calls=%fused_computation.3.clone.1 | loop fusion | flops 2359296 | bytes 9437185 | tf_op jit(solution)/shard_map/while/body/eval_jaxpr/add | solution.py:168
  230.4 2.7 convolution_bitcast_fusion.5
  235.6 5.2 %maximum_add_fusion.2 = f32[2,256,1536]{2,1,0:T(8,128)} fusion(f32[2,128,1536]{2,1,0:T(8,128)} %get-tuple-element.484, f32[2,128,1536]{2,1,0:T(8,128)} %get-tuple-element.485, f32[2,256,1536]{2,1,0:T(8,128)} %get-tuple-element.502, pred[]{:T(512)S(6)} %compare.14), kind=kLoop, calls=%fused_computation.3.clone.1 | loop fusion | flops 2359296 | bytes 9437185 | tf_op jit(solution)/shard_map/while/body/eval_jaxpr/add | solution.py:168
  248.8 2.7 convolution_bitcast_fusion.5
  254.0 5.2 %maximum_add_fusion.2 = f32[2,256,1536]{2,1,0:T(8,128)} fusion(f32[2,128,1536]{2,1,0:T(8,128)} %get-tuple-element.484, f32[2,128,1536]{2,1,0:T(8,128)} %get-tuple-element.485, f32[2,256,1536]{2,1,0:T(8,128)} %get-tuple-element.502, pred[]{:T(512)S(6)} %compare.14), kind=kLoop, calls=%fused_computation.3.clone.1 | loop fusion | flops 2359296 | bytes 9437185 | tf_op jit(solution)/shard_map/while/body/eval_jaxpr/add | solution.py:168
  272.3 5.2 %maximum_add_fusion.2 = f32[2,256,1536]{2,1,0:T(8,128)} fusion(f32[2,128,1536]{2,1,0:T(8,128)} %get-tuple-element.484, f32[2,128,1536]{2,1,0:T(8,128)} %get-tuple-element.485, f32[2,256,1536]{2,1,0:T(8,128)} %get-tuple-element.502, pred[]{:T(512)S(6)} %compare.14), kind=kLoop, calls=%fused_computation.3.clone.1 | loop fusion | flops 2359296 | bytes 9437185 | tf_op jit(solution)/shard_map/while/body/eval_jaxpr/add | solution.py:168
  277.5 8.8 %fusion.32 = bf16[2,128,1536]{1,2,0:T(8,128)(2,1)} fusion(f32[2,128,4608]{1,2,0:T(8,128)} %copy-done.3, f32[2,256,1536]{2,1,0:T(8,128)} %get-tuple-element.280, bf16[2,128,1536]{1,2,0:T(8,128)(2,1)} %fusion.31, f32[1536]{0:T(1024)S(1)} %reshape.237, f32[128,128]{1,0:T(8,128)} %get-tuple-element.392, f32[128,128]{1,0:T(8,128)} %get-tuple-element.391), kind=kOutput, calls=%fused_computation.69 | convolution fusion | flops 1209958400 | bytes 6428672 | tf_op jit(solution)/shard_map/if,sfd->sid/dot_general | solution.py:180
  (106 shorter events, 68.2 us)
Async XLA Ops:
  6.5 62.7 %copy-start = (bf16[1536,1152]{1,0:T(8,128)(2,1)S(1)}, bf16[1536,1152]{1,0:T(8,128)(2,1)}, u32[]{:S(2)}) copy-start(bf16[1536,1152]{1,0:T(8,128)(2,1)} %param.13) | copy-start | bytes 10616836
  6.5 22.6 %collective-permute-start = (bf16[2,128,1536]{2,1,0:T(8,128)(2,1)}, bf16[2,128,1536]{2,1,0:T(8,128)(2,1)}, u32[]{:S(2)}, u32[]{:S(2)}) collective-permute-start(bf16[2,128,1536]{2,1,0:T(8,128)(2,1)} %param.12), channel_id=1, source_target_pairs={{0,1},{1,2},{2,3},{3,0},{4,5},{5,6},{6,7},{7,4},{8,9},{9,10},{10,1... | collective-permute-start | bytes 2359304 | tf_op jit(solution)/shard_map/ppermute | solution.py:20
  8.1 36.6 %collective-permute-start.2 = (bf16[2,128,1536]{2,1,0:T(8,128)(2,1)}, bf16[2,128,1536]{2,1,0:T(8,128)(2,1)}, u32[]{:S(2)}, u32[]{:S(2)}) collective-permute-start(bf16[2,128,1536]{2,1,0:T(8,128)(2,1)} %param.12), channel_id=1, source_target_pairs={{1,0},{2,1},{3,2},{0,3},{5,4},{6,5},{7,6},{4,7},{9,8},{10,9},{11,1... | collective-permute-start | bytes 2359304 | tf_op jit(solution)/shard_map/ppermute | solution.py:22
  29.1 32.6 %collective-permute-start.1 = (bf16[2,128,1536]{2,1,0:T(8,128)(2,1)}, bf16[2,128,1536]{2,1,0:T(8,128)(2,1)}, u32[]{:S(2)}, u32[]{:S(2)}) collective-permute-start(bf16[2,128,1536]{2,1,0:T(8,128)(2,1)} %collective-permute-done), channel_id=1, source_target_pairs={{0,1},{1,2},{2,3},{3,0},{4,5},{5,6},{6,7},{7,4},{8,9},{9,10},{10,1... | collective-permute-start | bytes 2359304 | tf_op jit(solution)/shard_map/ppermute | solution.py:20
  76.8 4.7 %copy-start.5 = (s32[2,1]{0,1:T(1,128)S(1)}, s32[2,1]{0,1:T(1,128)}, u32[]{:S(2)}) copy-start(s32[2,1]{0,1:T(1,128)} %param.21) | copy-start | bytes 28
  76.8 56.4 %all-to-all-start = ((bf16[8,128,1152]{2,1,0:T(8,128)(2,1)}), bf16[8,128,1152]{2,1,0:T(8,128)(2,1)}, u32[]{:S(2)}, u32[]{:S(2)}) async-start(bf16[8,128,1152]{2,1,0:T(8,128)(2,1)} %bitcast.70), calls=%async_computation | async-start | bytes 4718592 | tf_op jit(solution)/shard_map/all_to_all | solution.py:118
  81.5 123.6 %all-gather.3.cloned.1.call-start = ((), (), s32[]{:S(2)}) async-start(), calls=%async_computation.1 | async-start | bytes 3932160 | tf_op jit(solution)/shard_map/all_gather | solution.py:171
  145.5 10.0 %collective-permute-start.3 = (bf16[2,1,4608]{2,0,1:T(2,128)(2,1)}, bf16[2,1,4608]{2,0,1:T(2,128)(2,1)}, u32[]{:S(2)}, u32[]{:S(2)}) collective-permute-start(bf16[2,1,4608]{2,0,1:T(2,128)(2,1)} %copy.21), channel_id=1, source_target_pairs={{0,4},{4,8},{8,12},{1,5},{5,9},{9,13},{2,6},{6,10},{10,14},{3,7},{... | collective-permute-start | bytes 55304 | tf_op jit(solution)/shard_map/ppermute | solution.py:37
  150.1 8.0 %collective-permute-start.4 = (bf16[2,1,4608]{2,0,1:T(2,128)(2,1)}, bf16[2,1,4608]{2,0,1:T(2,128)(2,1)}, u32[]{:S(2)}, u32[]{:S(2)}) collective-permute-start(bf16[2,1,4608]{2,0,1:T(2,128)(2,1)} %copy.23), channel_id=1, source_target_pairs={{4,0},{8,4},{12,8},{5,1},{9,5},{13,9},{6,2},{10,6},{14,10},{7,3},{... | collective-permute-start | bytes 55304 | tf_op jit(solution)/shard_map/ppermute | solution.py:39
  168.5 2.1 copy-start.3
  170.6 1.1 copy-start.4
  213.0 2.7 copy-start.1
  213.0 2.7 copy-start.2
  230.4 2.7 copy-start.1
  230.4 2.7 copy-start.2
  248.8 2.7 copy-start.1
  248.8 2.7 copy-start.2
  267.1 2.7 copy-start.1
  267.1 2.7 copy-start.2
Sparse Core Ops, SparseCore 0:
  171.8 26.8 all-gather.2
